TPU v7x, 32 devices: a whole 2x2x4 slice. The times are simulated.
32 devices in a mesh: dp: 8 (over z, y), tensor: 4 (over x, core).
Axes of the slice: x: 2, y: 2, z: 4, core: 2. Of those that a mesh axis runs over, the one named last changes fastest.
Arguments:
- hidden: bfloat16 [2048, 1024], P('dp'), may hold values from -6 to 6
- lengths: int32 [8, 16], P('dp'), may hold values from 1 to 64, 256 in all within a row
- w_qkv: bfloat16 [3, 1024, 1024], P(None, None, 'tensor')
- b_qkv: float32 [3, 1024], P(None, 'tensor'), may hold values from -3 to 3
- w_output: bfloat16 [1024, 1024], P('tensor'), may hold values from -0.1875 to 0.1875
- b_output: float32 [1024], replicated, may hold values from -3 to 3
- first_gain: float32 [1024], replicated, may hold values from 0.25 to 1.75
- first_shift: float32 [1024], replicated, may hold values from -3 to 3
- w_up: bfloat16 [1024, 4096], P(None, 'tensor'), may hold values from -0.1875 to 0.1875
- b_up: float32 [4096], P('tensor'), may hold values from -3 to 3
- w_down: bfloat16 [4096, 1024], P('tensor'), may hold values from -0.09375 to 0.09375
- b_down: float32 [1024], replicated, may hold values from -3 to 3
- second_gain: float32 [1024], replicated, may hold values from 0.25 to 1.75
- second_shift: float32 [1024], replicated, may hold values from -3 to 3
- index: bfloat16 [16384, 1024], P('dp', 'tensor'), may hold values from -6 to 6
- candidates: int32 [128, 64], replicated, may hold values from 0 to 16383, as said below
Outputs:
- states: bfloat16 [2048, 1024], P('dp')
- scores: float32 [128, 64], P('dp')
Inputs may be any that keep to these rules, and one draw needn't show every extreme that they name: `candidates`: each index of dp holds exactly 1024 of the 8192 named rows, counted with repetition.
All inputs are finite; a program needn't handle non-finite values.
Results may differ from a plain program's by a relative error of at most 0.014.
Values may be sent and summed in bfloat16 or wider, within the bound.
No kernel may reach another device: no remote copies, remote signals or barrier semaphores. Data moves between devices by JAX's collectives and lax.ppermute only.
A program may use at most 64 MiB of HBM per device.

v0:
```python
import math
import jax
import jax.numpy as jnp
from jax import lax
from jax.sharding import PartitionSpec as P

HEAD = 64


def layer_norm(values, gain, shift):
    centre = jnp.mean(values, axis=-1, keepdims=True)
    centred = values - centre
    spread = jnp.mean(centred * centred, axis=-1, keepdims=True)
    return centred * lax.rsqrt(spread + 1e-05) * gain + shift


def segment_of(pack_lengths, count):
    ends = jnp.cumsum(pack_lengths)
    position = jnp.arange(count, dtype=jnp.int32)
    return jnp.sum((position[:, None] >= ends[None, :]).astype(jnp.int32), axis=1)


def settle_attention(partial_value, residual, bias, gain, shift):
    total = lax.psum(partial_value.astype(jnp.bfloat16), "tensor").astype(jnp.float32)
    return layer_norm(total + bias + residual.astype(jnp.float32), gain, shift).astype(jnp.bfloat16)


def settle_forward(partial_value, residual, bias, gain, shift):
    total = lax.psum(partial_value.astype(jnp.bfloat16), "tensor").astype(jnp.float32)
    return layer_norm(total + bias + residual.astype(jnp.float32), gain, shift).astype(jnp.bfloat16)


def body(
    hidden,
    lengths,
    w_qkv,
    b_qkv,
    w_output,
    b_output,
    first_gain,
    first_shift,
    w_up,
    b_up,
    w_down,
    b_down,
    second_gain,
    second_shift,
    index,
    candidates,
):
    tokens_here = hidden.shape[0]
    local_width = w_qkv.shape[2]
    local_heads = local_width // HEAD
    projected = [
        jnp.dot(hidden, w_qkv[j], preferred_element_type=jnp.float32) + b_qkv[j] for j in range(3)
    ]
    queries = (projected[0] * 0.125).astype(jnp.bfloat16).reshape(tokens_here, local_heads, HEAD)
    keys = projected[1].astype(jnp.bfloat16).reshape(tokens_here, local_heads, HEAD)
    values = projected[2].astype(jnp.bfloat16).reshape(tokens_here, local_heads, HEAD)
    segment = segment_of(lengths[0], tokens_here)
    same = segment[:, None] == segment[None, :]
    logits = jnp.einsum("thd,shd->hts", queries, keys, preferred_element_type=jnp.float32)
    logits = jnp.where(same[None], logits, -1e30)
    top = jnp.max(logits, axis=-1, keepdims=True)
    expo = jnp.exp(logits - top)
    weights = (expo / jnp.sum(expo, axis=-1, keepdims=True)).astype(jnp.bfloat16)
    context = jnp.einsum("hts,shd->thd", weights, values, preferred_element_type=jnp.float32)
    context = context.astype(jnp.bfloat16).reshape(tokens_here, local_width)
    partial_value = jnp.dot(context, w_output, preferred_element_type=jnp.float32)
    attended = settle_attention(partial_value, hidden, b_output, first_gain, first_shift)
    activated = jax.nn.gelu(
        jnp.dot(attended, w_up, preferred_element_type=jnp.float32) + b_up, approximate=False
    ).astype(jnp.bfloat16)
    partial_value = jnp.dot(activated, w_down, preferred_element_type=jnp.float32)
    states = settle_forward(partial_value, attended, b_down, second_gain, second_shift)
    texts_here = lengths.shape[1]
    member = (segment[None, :] == jnp.arange(texts_here, dtype=jnp.int32)[:, None]).astype(
        jnp.bfloat16
    )
    pooled = (
        jnp.dot(member, states, preferred_element_type=jnp.float32)
        / lengths[0].astype(jnp.float32)[:, None]
    )
    unit = pooled * lax.rsqrt(jnp.sum(pooled * pooled, axis=-1, keepdims=True) + 1e-06)
    quarter = index.shape[1]
    unit_quarter = lax.dynamic_slice_in_dim(
        unit, lax.axis_index("tensor") * quarter, quarter, 1
    ).astype(jnp.bfloat16)
    row_base = lax.axis_index("dp") * index.shape[0]
    gathered = lax.all_gather(unit_quarter, "dp", axis=0, tiled=True)
    all_texts = candidates.shape[0]
    cand_count = candidates.shape[1]
    shard_rows = index.shape[0]
    block_rows = math.gcd(all_texts, 128)
    block_count = all_texts // block_rows
    local_rows = candidates - row_base
    row_ids = jnp.arange(shard_rows, dtype=jnp.int32)

    def score_block(packed):
        query_block, wanted = packed
        tile = lax.dot_general(
            query_block, index, (((1,), (1,)), ((), ())), preferred_element_type=jnp.float32
        )
        chosen = wanted[:, :, None] == row_ids[None, None, :]
        return jnp.sum(jnp.where(chosen, tile[:, None, :], 0.0), axis=2)

    partial_scores = lax.map(
        score_block,
        (
            gathered.reshape(block_count, block_rows, quarter),
            local_rows.reshape(block_count, block_rows, cand_count),
        ),
    )
    partial_scores = partial_scores.reshape(all_texts, cand_count)
    slice_scores = lax.psum_scatter(
        partial_scores, ("dp", "tensor"), scatter_dimension=0, tiled=True
    )
    scores = lax.all_gather(slice_scores, "tensor", axis=0, tiled=True)
    return (states, scores)


def solution(mesh):
    placed = (
        P("dp", None),
        P("dp", None),
        P(None, None, "tensor"),
        P(None, "tensor"),
        P("tensor", None),
        P(),
        P(),
        P(),
        P(None, "tensor"),
        P("tensor"),
        P("tensor", None),
        P(),
        P(),
        P(),
        P("dp", "tensor"),
        P(),
    )
    return jax.shard_map(
        body, mesh=mesh, in_specs=placed, out_specs=(P("dp", None), P("dp", None)), check_vma=False
    )
```

profile of v0, /device:TPU:15, one launch (start us, length us, event | category | flops | bytes accessed | tf_op | source)
XLA Modules:
  0.0 194.1 jit_solution(16302811454098410085)
XLA Ops:
  7.2 0.0 all-reduce.4.cloned.1.call-start
  7.2 0.9 fusion.90
  8.1 1.6 fusion.6
  9.7 1.6 fusion.5
  11.3 0.1 copy.27
  11.4 0.1 reduce
  11.6 0.1 convert_reduce_fusion
  11.6 0.1 broadcast_compare_fusion
  11.8 1.3 convolution_select_fusion
  13.1 0.5 fusion.91
  13.6 1.4 fusion.4
  15.1 2.0 %convolution_convert_fusion.2 = bf16[4,64,256]{2,1,0:T(8,128)(2,1)S(1)} fusion(bf16[256,4,64]{0,2,1:T(8,128)(2,1)S(1)} %bitcast.51, f32[4,256]{1,0:T(4,128)S(1)} %fusion.91, f32[4,256,256]{1,2,0:T(8,128)} %convolution_select_fusion), kind=kOutput, calls=%fused_computation.14 | convolution fusion | flops 34407680 | bytes 1314816 | tf_op jit(solution)/shard_map/hts,shd->thd/dot_general | solution.py:67
  17.1 1.1 convolution_convert_fusion
  18.2 0.0 all-reduce.6.cloned.1.call-start
  18.3 32.6 %all-reduce.4.cloned.1.call-done = bf16[256,1024]{1,0:T(8,128)(2,1)} async-done(((bf16[256,1024]{1,0:T(8,128)(2,1)}), bf16[256,1024]{1,0:T(8,128)(2,1)}) %all-reduce.4.cloned.1.call-update) | async-done | bytes 524304 | tf_op jit(solution)/shard_map/psum | solution.py:24
  50.8 1.4 fusion.17
  52.2 1.4 multiply_reduce_fusion.1
  53.6 0.3 add_convert_fusion.1
  54.0 5.9 %convolution_convert_fusion.1 = bf16[256,1024]{1,0:T(8,128)(2,1)} fusion(bf16[1024,1024]{1,0:T(8,128)(2,1)S(1)} %copy-done, bf16[256,1024]{1,0:T(8,128)(2,1)S(1)} %add_convert_fusion.1, bf16[1024,1024]{1,0:T(8,128)(2,1)} %param.24, f32[1024]{0:T(1024)S(1)} %copy-done.15), kind=kOutput, calls=%fused_computation.9 | convolution fusion | flops 1091305472 | bytes 5246976 | tf_op jit(solution)/shard_map/dot_general | solution.py:74
  59.9 0.1 copy.29
  60.1 33.2 %all-reduce.6.cloned.1.call-done = bf16[256,1024]{1,0:T(8,128)(2,1)} async-done(((bf16[256,1024]{1,0:T(8,128)(2,1)}), bf16[256,1024]{1,0:T(8,128)(2,1)}) %all-reduce.6.cloned.1.call-update) | async-done | bytes 524304 | tf_op jit(solution)/shard_map/psum | solution.py:29
  93.3 1.4 fusion.18
  94.7 1.4 multiply_reduce_fusion
  96.1 0.3 add_convert_fusion
  96.4 0.3 multiply_reduce_fusion.2
  96.7 0.1 fusion.56
  96.8 21.9 %all_gather.6 = bf16[128,256]{1,0:T(8,128)(2,1)S(1)} all-gather(bf16[16,256]{1,0:T(8,128)(2,1)S(1)} %fusion.56), channel_id=1, replica_groups=mesh['dp'=8,'tensor'=4] {'dp'}, dimensions={0}, use_global_device_ids=true | all-gather | bytes 73728 | tf_op jit(solution)/shard_map/all_gather | solution.py:90
  118.7 0.5 fusion.92
  119.2 10.9 %select_reduce_fusion = f32[128,64]{1,0:T(8,128)S(1)} fusion(f32[128,2048]{1,0:T(8,128)S(1)} %fusion.92, s32[128,64]{1,0:T(8,128)S(1)} %copy.29), kind=kLoop, calls=%fused_computation.1 | loop fusion | flops 50323456 | bytes 1114112 | tf_op jit(solution)/shard_map/while/body/eval_jaxpr/reduce_sum | solution.py:105
  130.1 49.1 %all-reduce = f32[128,64]{1,0:T(8,128)S(1)} all-reduce(f32[128,64]{1,0:T(8,128)S(1)} %select_reduce_fusion), channel_id=2, replica_groups=mesh['dp'=8,'tensor'=4] {'dp','tensor'}, use_global_device_ids=true, to_apply=%region_12.13.clone | all-reduce | flops 8192 | bytes 65536
  179.2 7.4 %all-gather = f32[4,4,64]{2,1,0:T(4,128)S(1)} all-gather(f32[1,4,64]{2,1,0:T(4,128)S(1)} %dynamic-slice_bitcast_fusion), channel_id=1, replica_groups=mesh['dp'=8,'tensor'=4] {'tensor'}, dimensions={0}, use_global_device_ids=true | all-gather | bytes 5120 | tf_op jit(solution)/shard_map/all_gather | solution.py:118
  186.6 0.6 copy.34
  (43 shorter events, 0.2 us)
Async XLA Ops:
  7.2 46.8 %copy-start = (bf16[1024,1024]{1,0:T(8,128)(2,1)S(1)}, bf16[1024,1024]{1,0:T(8,128)(2,1)}, u32[]{:S(2)}) copy-start(bf16[1024,1024]{1,0:T(8,128)(2,1)} %param.26) | copy-start | bytes 6291460
  7.2 4.1 %copy-start.14 = (s32[1,16]{1,0:T(1,128)S(1)}, s32[1,16]{1,0:T(1,128)}, u32[]{:S(2)}) copy-start(s32[1,16]{1,0:T(1,128)} %param.17) | copy-start | bytes 196
  7.2 43.6 %all-reduce.4.cloned.1.call-start = ((), (), s32[]{:S(2)}) async-start(), calls=%async_computation | async-start | bytes 1048576 | tf_op jit(solution)/shard_map/psum | solution.py:24
  9.7 4.0 %copy-start.1 = (bf16[256,1024]{1,0:T(8,128)(2,1)S(1)}, bf16[256,1024]{1,0:T(8,128)(2,1)}, u32[]{:S(2)}) copy-start(bf16[256,1024]{1,0:T(8,128)(2,1)} %param.16) | copy-start | bytes 1572868
  15.0 2.0 %copy-start.6 = (bf16[256,1024]{1,0:T(8,128)(2,1)S(1)}, bf16[256,1024]{1,0:T(8,128)(2,1)}, u32[]{:S(2)}) copy-start(bf16[256,1024]{1,0:T(8,128)(2,1)} %param.20) | copy-start | bytes 1572868
  15.0 35.8 %copy-start.7 = (f32[1024]{0:T(1024)S(1)}, f32[1024]{0:T(1024)}, u32[]{:S(2)}) copy-start(f32[1024]{0:T(1024)} %param.21) | copy-start | bytes 12292
  17.0 36.6 %copy-start.10 = (f32[1024]{0:T(1024)S(1)}, f32[1024]{0:T(1024)}, u32[]{:S(2)}) copy-start(f32[1024]{0:T(1024)} %param.23) | copy-start | bytes 12292
  17.0 36.5 %copy-start.11 = (f32[1024]{0:T(1024)S(1)}, f32[1024]{0:T(1024)}, u32[]{:S(2)}) copy-start(f32[1024]{0:T(1024)} %param.22) | copy-start | bytes 12292
  18.2 35.8 %copy-start.15 = (f32[1024]{0:T(1024)S(1)}, f32[1024]{0:T(1024)}, u32[]{:S(2)}) copy-start(f32[1024]{0:T(1024)} %param.25) | copy-start | bytes 12292
  18.2 75.1 %all-reduce.6.cloned.1.call-start = ((), (), s32[]{:S(2)}) async-start(), calls=%async_computation.1 | async-start | bytes 1048576 | tf_op jit(solution)/shard_map/psum | solution.py:29
  50.8 2.8 %copy-start.3 = (bf16[256,1024]{1,0:T(8,128)(2,1)S(1)}, bf16[256,1024]{1,0:T(8,128)(2,1)}, u32[]{:S(2)}) copy-start(bf16[256,1024]{1,0:T(8,128)(2,1)} %all-reduce.4.cloned.1.call-done) | copy-start | bytes 1572868
  53.9 6.0 %copy-start.9 = (s32[128,64]{0,1:T(8,128)S(1)}, s32[128,64]{0,1:T(8,128)}, u32[]{:S(2)}) copy-start(s32[128,64]{0,1:T(8,128)} %param.31) | copy-start | bytes 98308
  54.0 39.3 %copy-start.8 = (f32[1024]{0:T(1024)S(1)}, f32[1024]{0:T(1024)}, u32[]{:S(2)}) copy-start(f32[1024]{0:T(1024)} %param.27) | copy-start | bytes 12292
  59.9 36.2 %copy-start.12 = (f32[1024]{0:T(1024)S(1)}, f32[1024]{0:T(1024)}, u32[]{:S(2)}) copy-start(f32[1024]{0:T(1024)} %param.29) | copy-start | bytes 12292
  59.9 36.2 %copy-start.13 = (f32[1024]{0:T(1024)S(1)}, f32[1024]{0:T(1024)}, u32[]{:S(2)}) copy-start(f32[1024]{0:T(1024)} %param.28) | copy-start | bytes 12292
  93.3 2.8 %copy-start.2 = (bf16[256,1024]{1,0:T(8,128)(2,1)S(1)}, bf16[256,1024]{1,0:T(8,128)(2,1)}, u32[]{:S(2)}) copy-start(bf16[256,1024]{1,0:T(8,128)(2,1)} %all-reduce.6.cloned.1.call-done) | copy-start | bytes 1572868
  93.3 25.4 %copy-start.5 = (bf16[2048,256]{1,0:T(8,128)(2,1)S(1)}, bf16[2048,256]{1,0:T(8,128)(2,1)}, u32[]{:S(2)}) copy-start(bf16[2048,256]{1,0:T(8,128)(2,1)} %param.30) | copy-start | bytes 3145732
  96.4 90.8 %copy-start.4 = (bf16[256,1024]{1,0:T(8,128)(2,1)}, bf16[256,1024]{1,0:T(8,128)(2,1)S(1)}, u32[]{:S(2)}) copy-start(bf16[256,1024]{1,0:T(8,128)(2,1)S(1)} %add_convert_fusion) | copy-start | bytes 1572868
Sparse Core Ops, SparseCore 0:
  18.3 32.4 all-reduce.3
  60.0 33.1 all-reduce.5
where the time goes:
time: 195 us; the launch traced here: 194 us
  blocking collectives  78.4 us (40%)
  waiting for transfers between devices  65.8 us (34%)
  other arithmetic  17.6 us (9%)
  matrix products  16.2 us (8%)
  between operations  14.3 us (7%)
    unnamed x1, blocking collectives  49.1 us
    psum x1, waiting for transfers between devices, settle_forward(): lax.psum(partial_value.astype(jnp.bfloat16), 'tensor').astype(jnp.float32)  33.2 us
    psum x1, waiting for transfers between devices, settle_attention(): lax.psum(partial_value.astype(jnp.bfloat16), 'tensor').astype(jnp.float32)  32.6 us
    all_gather x1, blocking collectives, body(): gathered = lax.all_gather(unit_quarter, 'dp', axis=0, tiled=True)  21.9 us
    reduce_sum x1, other arithmetic, score_block(): return jnp.sum(jnp.where(chosen, tile[:, None, :], 0.0), axis=2)  10.9 us
    all_gather x1, blocking collectives, body(): scores = lax.all_gather(slice_scores, 'tensor', axis=0, tiled=True)  7.4 us
    dot_general x1, matrix products, body(): jnp.dot(activated, w_down, preferred_element_type=jnp.float32)  5.9 us
    dot_general x3, matrix products, body(): jnp.dot(hidden, w_qkv[j], preferred_element_type=jnp.float32) + b_qkv[j]  4.58 us
  transfers between devices with their start and end apart: 2, of which 2 were waited for; matrix products, arithmetic and copies ran while one was open for 0% of the time, Pallas kernels for 0%

commit v1 on v0

--- a/solution.py
+++ b/solution.py
@@ -21,7 +21,9 @@
 
 
 def settle_attention(partial_value, residual, bias, gain, shift):
-    total = lax.psum(partial_value.astype(jnp.bfloat16), "tensor").astype(jnp.float32)
+    total = jnp.sum(lax.all_gather(partial_value.astype(jnp.bfloat16), "tensor"), axis=0).astype(
+        jnp.float32
+    )
     return layer_norm(total + bias + residual.astype(jnp.float32), gain, shift).astype(jnp.bfloat16)
 
 

time: 195 us -> 184 us (0.944)
  waiting for transfers between devices: 65.8 us -> 55.2 us
    psum x1 -> x0, waiting for transfers between devices: 32.6 us -> none  [settle_attention(): lax.psum(partial_value.astype(jnp.bfloat16), 'tensor').astype(jnp.float32)]
    all_gather x0 -> x1, waiting for transfers between devices: none -> 23.3 us  [settle_attention(): lax.all_gather(partial_value.astype(jnp.bfloat16), 'tensor')]
    reduce_sum x0 -> x1, other arithmetic: none -> 2.05 us  [settle_attention(): jnp.sum(lax.all_gather(partial_value.astype(jnp.bfloat16), 'tensor'), axi...]
where the time goes in v1:
time: 184 us
  blocking collectives  78.3 us (43%)
  waiting for transfers between devices  55.2 us (30%)
  other arithmetic  17.4 us (9%)
  matrix products  16.2 us (9%)
  between operations  14.3 us (8%)
  local copies, waits for them, and re-layouts  2.12 us (1%)
    unnamed x1, blocking collectives  49 us
    psum x1, waiting for transfers between devices, settle_forward(): lax.psum(partial_value.astype(jnp.bfloat16), 'tensor').astype(jnp.float32)  31.9 us
    all_gather x1, waiting for transfers between devices, settle_attention(): lax.all_gather(partial_value.astype(jnp.bfloat16), 'tensor')  23.3 us
    all_gather x1, blocking collectives, body(): gathered = lax.all_gather(unit_quarter, 'dp', axis=0, tiled=True)  21.9 us
    reduce_sum x1, other arithmetic, score_block(): return jnp.sum(jnp.where(chosen, tile[:, None, :], 0.0), axis=2)  10.9 us
    all_gather x1, blocking collectives, body(): scores = lax.all_gather(slice_scores, 'tensor', axis=0, tiled=True)  7.4 us
    dot_general x1, matrix products, body(): jnp.dot(activated, w_down, preferred_element_type=jnp.float32)  5.93 us
    dot_general x3, matrix products, body(): jnp.dot(hidden, w_qkv[j], preferred_element_type=jnp.float32) + b_qkv[j]  4.59 us
  transfers between devices with their start and end apart: 2, of which 2 were waited for; matrix products, arithmetic and copies ran while one was open for 0% of the time, Pallas kernels for 0%

profile of v1, /device:TPU:15, one launch (start us, length us, event | category | flops | bytes accessed | tf_op | source)
XLA Modules:
  0.0 183.7 jit_solution(15904136766832572912)
XLA Ops:
  7.2 0.9 fusion.90
  8.1 1.6 fusion.6
  9.7 1.6 fusion.5
  11.3 0.1 copy.27
  11.4 0.1 reduce.1
  11.6 0.1 convert_reduce_fusion
  11.6 0.1 broadcast_compare_fusion
  11.8 1.3 convolution_select_fusion
  13.1 0.5 fusion.91
  13.6 1.4 fusion.4
  15.0 2.0 %convolution_convert_fusion.2 = bf16[4,64,256]{2,1,0:T(8,128)(2,1)S(1)} fusion(bf16[256,4,64]{0,2,1:T(8,128)(2,1)S(1)} %bitcast.53, f32[4,256]{1,0:T(4,128)S(1)} %fusion.91, f32[4,256,256]{1,2,0:T(8,128)} %convolution_select_fusion), kind=kOutput, calls=%fused_computation.14 | convolution fusion | flops 34407680 | bytes 1314816 | tf_op jit(solution)/shard_map/hts,shd->thd/dot_general | solution.py:69
  17.0 1.1 convolution_convert_fusion
  18.2 23.3 %all-gather.4.cloned.1.call-done = bf16[1024,1024]{1,0:T(8,128)(2,1)} async-done(((bf16[256,1024]{1,0:T(8,128)(2,1)}), bf16[1024,1024]{1,0:T(8,128)(2,1)}) %all-gather.4.cloned.1.call-update) | async-done | bytes 2097168 | tf_op jit(solution)/shard_map/all_gather | solution.py:24
  41.5 2.0 %reduce_sum.87 = bf16[256,1024]{1,0:T(8,128)(2,1)S(1)} reduce(bf16[4,256,1024]{2,1,0:T(8,128)(2,1)} %bitcast.42, bf16[]{:T(256)} %constant.49.clone.1), dimensions={0}, to_apply=%region_4.5 | reduce | flops 786432 | bytes 2621442 | tf_op jit(solution)/shard_map/reduce_sum | solution.py:24
  43.6 0.3 fusion.17
  43.9 0.3 multiply_reduce_fusion.1
  44.2 0.4 copy-done.2
  44.6 0.3 add_convert_fusion.1
  45.0 5.9 %convolution_convert_fusion.1 = bf16[256,1024]{1,0:T(8,128)(2,1)} fusion(bf16[1024,1024]{1,0:T(8,128)(2,1)S(1)} %copy-done, bf16[256,1024]{1,0:T(8,128)(2,1)S(1)} %add_convert_fusion.1, bf16[1024,1024]{1,0:T(8,128)(2,1)} %param.24, f32[1024]{0:T(1024)S(1)} %copy-done.15), kind=kOutput, calls=%fused_computation.9 | convolution fusion | flops 1091305472 | bytes 5246976 | tf_op jit(solution)/shard_map/dot_general | solution.py:76
  51.0 0.1 copy.29
  51.1 31.9 %all-reduce.3.cloned.1.call-done = bf16[256,1024]{1,0:T(8,128)(2,1)} async-done(((bf16[256,1024]{1,0:T(8,128)(2,1)}), bf16[256,1024]{1,0:T(8,128)(2,1)}) %all-reduce.3.cloned.1.call-update) | async-done | bytes 524304 | tf_op jit(solution)/shard_map/psum | solution.py:31
  83.0 1.4 fusion.18
  84.4 1.4 multiply_reduce_fusion
  85.8 0.3 add_convert_fusion
  86.2 0.3 multiply_reduce_fusion.2
  86.5 0.1 fusion.56
  86.6 21.9 %all_gather.14 = bf16[128,256]{1,0:T(8,128)(2,1)S(1)} all-gather(bf16[16,256]{1,0:T(8,128)(2,1)S(1)} %fusion.56), channel_id=1, replica_groups=mesh['dp'=8,'tensor'=4] {'dp'}, dimensions={0}, use_global_device_ids=true | all-gather | bytes 73728 | tf_op jit(solution)/shard_map/all_gather | solution.py:92
  108.5 0.5 fusion.92
  108.9 10.9 %select_reduce_fusion = f32[128,64]{1,0:T(8,128)S(1)} fusion(f32[128,2048]{1,0:T(8,128)S(1)} %fusion.92, s32[128,64]{1,0:T(8,128)S(1)} %copy.29), kind=kLoop, calls=%fused_computation.1 | loop fusion | flops 50323456 | bytes 1114112 | tf_op jit(solution)/shard_map/while/body/eval_jaxpr/reduce_sum | solution.py:107
  119.8 49.0 %all-reduce = f32[128,64]{1,0:T(8,128)S(1)} all-reduce(f32[128,64]{1,0:T(8,128)S(1)} %select_reduce_fusion), channel_id=3, replica_groups=mesh['dp'=8,'tensor'=4] {'dp','tensor'}, use_global_device_ids=true, to_apply=%region_12.13.clone | all-reduce | flops 8192 | bytes 65536
  168.9 7.4 %all-gather.1 = f32[4,4,64]{2,1,0:T(4,128)S(1)} all-gather(f32[1,4,64]{2,1,0:T(4,128)S(1)} %dynamic-slice_bitcast_fusion), channel_id=1, replica_groups=mesh['dp'=8,'tensor'=4] {'tensor'}, dimensions={0}, use_global_device_ids=true | all-gather | bytes 5120 | tf_op jit(solution)/shard_map/all_gather | solution.py:120
  176.3 0.6 copy.33
  (44 shorter events, 0.3 us)
Async XLA Ops:
  7.2 37.8 %copy-start = (bf16[1024,1024]{1,0:T(8,128)(2,1)S(1)}, bf16[1024,1024]{1,0:T(8,128)(2,1)}, u32[]{:S(2)}) copy-start(bf16[1024,1024]{1,0:T(8,128)(2,1)} %param.26) | copy-start | bytes 6291460
  7.2 4.1 %copy-start.14 = (s32[1,16]{1,0:T(1,128)S(1)}, s32[1,16]{1,0:T(1,128)}, u32[]{:S(2)}) copy-start(s32[1,16]{1,0:T(1,128)} %param.17) | copy-start | bytes 196
  7.2 34.3 %all-gather.4.cloned.1.call-start = ((), (), s32[]{:S(2)}) async-start(), calls=%async_computation.1 | async-start | bytes 2621440 | tf_op jit(solution)/shard_map/all_gather | solution.py:24
  9.7 4.0 %copy-start.1 = (bf16[256,1024]{1,0:T(8,128)(2,1)S(1)}, bf16[256,1024]{1,0:T(8,128)(2,1)}, u32[]{:S(2)}) copy-start(bf16[256,1024]{1,0:T(8,128)(2,1)} %param.16) | copy-start | bytes 1572868
  15.0 2.0 %copy-start.6 = (bf16[256,1024]{1,0:T(8,128)(2,1)S(1)}, bf16[256,1024]{1,0:T(8,128)(2,1)}, u32[]{:S(2)}) copy-start(bf16[256,1024]{1,0:T(8,128)(2,1)} %param.20) | copy-start | bytes 1572868
  17.0 26.5 %copy-start.7 = (f32[1024]{0:T(1024)S(1)}, f32[1024]{0:T(1024)}, u32[]{:S(2)}) copy-start(f32[1024]{0:T(1024)} %param.21) | copy-start | bytes 12292
  18.2 64.8 %all-reduce.3.cloned.1.call-start = ((), (), s32[]{:S(2)}) async-start(), calls=%async_computation | async-start | bytes 1048576 | tf_op jit(solution)/shard_map/psum | solution.py:31
  41.5 2.7 %copy-start.10 = (f32[1024]{0:T(1024)S(1)}, f32[1024]{0:T(1024)}, u32[]{:S(2)}) copy-start(f32[1024]{0:T(1024)} %param.23) | copy-start | bytes 12292
  41.5 2.7 %copy-start.11 = (f32[1024]{0:T(1024)S(1)}, f32[1024]{0:T(1024)}, u32[]{:S(2)}) copy-start(f32[1024]{0:T(1024)} %param.22) | copy-start | bytes 12292
  43.6 1.0 copy-start.2
  43.6 1.4 copy-start.15
  45.0 6.0 %copy-start.9 = (s32[128,64]{0,1:T(8,128)S(1)}, s32[128,64]{0,1:T(8,128)}, u32[]{:S(2)}) copy-start(s32[128,64]{0,1:T(8,128)} %param.31) | copy-start | bytes 98308
  45.0 38.0 %copy-start.8 = (f32[1024]{0:T(1024)S(1)}, f32[1024]{0:T(1024)}, u32[]{:S(2)}) copy-start(f32[1024]{0:T(1024)} %param.27) | copy-start | bytes 12292
  50.9 34.9 %copy-start.12 = (f32[1024]{0:T(1024)S(1)}, f32[1024]{0:T(1024)}, u32[]{:S(2)}) copy-start(f32[1024]{0:T(1024)} %param.29) | copy-start | bytes 12292
  50.9 34.9 %copy-start.13 = (f32[1024]{0:T(1024)S(1)}, f32[1024]{0:T(1024)}, u32[]{:S(2)}) copy-start(f32[1024]{0:T(1024)} %param.28) | copy-start | bytes 12292
  83.0 2.8 %copy-start.3 = (bf16[256,1024]{1,0:T(8,128)(2,1)S(1)}, bf16[256,1024]{1,0:T(8,128)(2,1)}, u32[]{:S(2)}) copy-start(bf16[256,1024]{1,0:T(8,128)(2,1)} %all-reduce.3.cloned.1.call-done) | copy-start | bytes 1572868
  83.0 25.4 %copy-start.5 = (bf16[2048,256]{1,0:T(8,128)(2,1)S(1)}, bf16[2048,256]{1,0:T(8,128)(2,1)}, u32[]{:S(2)}) copy-start(bf16[2048,256]{1,0:T(8,128)(2,1)} %param.30) | copy-start | bytes 3145732
  86.2 90.7 %copy-start.4 = (bf16[256,1024]{1,0:T(8,128)(2,1)}, bf16[256,1024]{1,0:T(8,128)(2,1)S(1)}, u32[]{:S(2)}) copy-start(bf16[256,1024]{1,0:T(8,128)(2,1)S(1)} %add_convert_fusion) | copy-start | bytes 1572868
Sparse Core Ops, SparseCore 0:
  18.3 23.1 all-gather.3
  51.1 31.8 all-reduce.2
